TPU v7x, 32 devices: a whole 2x2x4 slice. The times are simulated.
32 devices in a mesh: tm: 16 (over z, x, core), doc: 2 (over y).
Axes of the slice: x: 2, y: 2, z: 4, core: 2. Of those that a mesh axis runs over, the one named last changes fastest.
Arguments:
- beta: float32 [16, 4096, 128], P('tm', 'doc'), may hold values from -6 to 260
- word_ids: int32 [16, 8, 128], P('tm', 'doc'), may hold values from 0 to 4095
- word_counts: int32 [16, 8, 128], P('tm', 'doc'), may hold values from 1 to 8
- block_slot: int32 [32], replicated, may hold values from 0 to 31, each once
- topic_prior: float32 [128], replicated, may hold values from 0.05 to 0.5
- drift_var: float32 [128], replicated, may hold values from 0.0005 to 0.05
- obs_precision: float32 [16, 128], replicated, may hold values from 0.01 to 4
Outputs:
- smoothed_means: float32 [16, 4096, 128], P('tm', 'doc')
- doc_topics: float32 [16, 8, 128], P('tm', 'doc')
Inputs may be any that keep to these rules, and one draw needn't show every extreme that they name: `block_slot`: each block has its own position.
All inputs are finite; a program needn't handle non-finite values.
Results may differ from a plain program's by a relative error of at most 0.0012.
The roundings to bfloat16 on the way count: a program that leaves them out, or rounds other values in their place, can miss the bound.
Values may be sent and summed in bfloat16 or wider, within the bound.
No kernel may reach another device: no remote copies, remote signals or barrier semaphores. Data moves between devices by JAX's collectives and lax.ppermute only.
A program may use at most 192 MiB of HBM per device.

v0:
```python
import jax
import jax.numpy as jnp
from jax import lax
from jax.sharding import PartitionSpec as P

K = 128
BLOCK = 128
EITERS = 4
init_variance = 4.0


def variance_tables(obs_precision, drift_var):

    def forward_step(prior_var, precision):
        denominator = 1.0 + prior_var * precision
        gain_now = prior_var * precision / denominator
        filt_var = prior_var / denominator
        return (filt_var + drift_var, (gain_now, filt_var))

    start_var = jnp.full(drift_var.shape, init_variance, dtype=jnp.float32)
    last_var, (gains, filt_vars) = lax.scan(forward_step, start_var, obs_precision)

    def backward_step(info_next, precision):
        merged = info_next + precision
        shrink = 1.0 / (1.0 + drift_var * merged)
        info_now = merged * shrink
        return (info_now, (shrink, info_now))

    zero_info = jnp.zeros(drift_var.shape, dtype=jnp.float32)
    last_info, (shrinks, infos) = lax.scan(
        backward_step, zero_info, obs_precision[1:], reverse=True
    )
    shrinks = jnp.concatenate([shrinks, jnp.ones_like(zero_info)[None]], axis=0)
    infos = jnp.concatenate([infos, zero_info[None]], axis=0)
    return (gains, filt_vars, shrinks, infos)


def e_step(looked, word_counts, topic_prior):
    counts_float = word_counts.astype(jnp.float32)
    doc_topics = topic_prior + jnp.sum(counts_float, axis=-1, keepdims=True) / K
    scores = looked.astype(jnp.float32)
    for sweep in range(EITERS):
        resp = jax.nn.softmax(lax.digamma(doc_topics)[..., None, :] + scores, axis=-1)
        doc_topics = topic_prior + jnp.sum(counts_float[..., None] * resp, axis=-2)
    weighted = (counts_float[..., None] * resp).astype(jnp.bfloat16)
    return (doc_topics, weighted)


def body(beta, word_ids, word_counts, block_slot, topic_prior, drift_var, obs_precision):
    local_beta = beta[0]
    own_words = local_beta.shape[0]
    topics = local_beta.shape[1]
    doc_devices = lax.axis_size("doc")
    doc_place = lax.axis_index("doc")
    local_peak = jnp.max(local_beta, axis=0)
    local_total = jnp.sum(jnp.exp(local_beta - local_peak), axis=0)
    slot_ids = word_ids[0]
    local_docs = slot_ids.shape[0]
    slot_width = slot_ids.shape[1]
    columns = jnp.take(block_slot, slot_ids // BLOCK) * BLOCK + slot_ids % BLOCK
    all_columns = lax.all_gather(columns, "doc", axis=0, tiled=True)
    all_counts = lax.all_gather(word_counts[0], "doc", axis=0, tiled=True)
    peaks = lax.all_gather(local_peak, "doc")
    totals = lax.all_gather(local_total, "doc")
    peak_value = jnp.max(peaks, axis=0)
    total_value = jnp.sum(totals * jnp.exp(peaks - peak_value), axis=0)
    normalizer = peak_value + jnp.log(total_value)
    flat_columns = all_columns.reshape(-1)
    local_columns = flat_columns - doc_place * own_words
    inside = (local_columns >= 0) & (local_columns < own_words)
    picked = jnp.take(local_beta, jnp.clip(local_columns, 0, own_words - 1), axis=0)
    partial = jnp.where(
        inside[:, None], (picked - normalizer).astype(jnp.bfloat16), jnp.zeros((), jnp.bfloat16)
    )
    looked = lax.psum(partial, "doc").reshape(local_docs * doc_devices, slot_width, topics)
    doc_topics_all, weighted = e_step(looked, all_counts, topic_prior)
    doc_topics = lax.dynamic_slice_in_dim(doc_topics_all, doc_place * local_docs, local_docs, 0)
    flat_weighted = weighted.reshape(-1, topics)
    row_words = lax.iota(jnp.int32, own_words)
    marks = (row_words[:, None] == local_columns[None, :]).astype(jnp.bfloat16)
    counts = jnp.dot(marks, flat_weighted, preferred_element_type=jnp.float32)
    pseudo = local_beta + jnp.log1p(counts)
    gains, filt_vars, shrinks, infos = variance_tables(obs_precision, drift_var)
    years_total = obs_precision.shape[0]
    pulls = filt_vars / (filt_vars + drift_var)
    pulls = pulls.at[-1].set(0.0)
    years = lax.axis_size("tm")
    chunk = own_words // years
    by_year = lax.all_to_all(
        pseudo.reshape(years, chunk, topics), "tm", split_axis=0, concat_axis=0, tiled=True
    )

    def filter_step(mean_prev, inputs):
        gain_now, pseudo_now = inputs
        mean_now = (1.0 - gain_now) * mean_prev + gain_now * pseudo_now
        return (mean_now, mean_now)

    zero_mean = jnp.zeros((chunk, topics), dtype=jnp.float32)
    last_mean, filtered = lax.scan(
        filter_step, zero_mean, (gains[:, None, :], by_year), unroll=True
    )

    def smooth_step(mean_next, inputs):
        pull_now, filt_now = inputs
        mean_now = pull_now * mean_next + (1.0 - pull_now) * filt_now
        return (mean_now, mean_now)

    first_mean, smoothed = lax.scan(
        smooth_step, zero_mean, (pulls[:, None, :], filtered), reverse=True, unroll=True
    )
    back = lax.all_to_all(smoothed, "tm", split_axis=0, concat_axis=0, tiled=True)
    return (back.reshape(own_words, topics)[None], doc_topics[None])


def solution(mesh):
    in_specs = (
        P("tm", "doc", None),
        P("tm", "doc", None),
        P("tm", "doc", None),
        P(),
        P(),
        P(),
        P(),
    )
    out_specs = (P("tm", "doc", None), P("tm", "doc", None))
    return jax.shard_map(body, mesh=mesh, in_specs=in_specs, out_specs=out_specs, check_vma=False)
```

profile of v0, /device:TPU:9, one launch (start us, length us, event | category | flops | bytes accessed | tf_op | source)
XLA Modules:
  0.0 144.6 jit_solution(16217126004983186146)
XLA Ops:
  7.2 1.6 %reduce_max.54 = f32[128]{0:T(128)S(1)} reduce(f32[1,2048,128]{2,1,0:T(8,128)} %param.11, f32[]{:T(128)} %constant.154.clone.1), dimensions={0,1}, to_apply=%region_3.4 | reduce | flops 262016 | bytes 1049092 | tf_op jit(solution)/shard_map/reduce_max | solution.py:55
  9.1 3.1 %all-gather.5 = f32[2,1,128]{2,1,0:T(1,128)S(1)} all-gather(f32[1,1,128]{2,1,0:T(1,128)S(1)} %bitcast.281), channel_id=4, replica_groups=mesh['tm'=16,'doc'=2] {'doc'}, dimensions={0}, use_global_device_ids=true | all-gather | bytes 1536 | tf_op jit(solution)/shard_map/all_gather | solution.py:64
  12.2 3.1 %all-gather.4 = f32[2,1,128]{2,1,0:T(1,128)S(1)} all-gather(f32[1,1,128]{2,1,0:T(1,128)S(1)} %bitcast.278), channel_id=3, replica_groups=mesh['tm'=16,'doc'=2] {'doc'}, dimensions={0}, use_global_device_ids=true | all-gather | bytes 1536 | tf_op jit(solution)/shard_map/all_gather | solution.py:63
  15.4 3.3 %gather_fusion = s32[512]{0:T(512)S(1)} fusion(s32[32]{0:T(128)S(1)} %copy-done, s32[1024]{0:T(1024)S(1)} %pad_clamp_fusion), kind=kCustom, calls=%fused_computation | custom fusion | bytes 6144 | tf_op jit(solution)/shard_map/jit(_take)/gather | solution.py:60
  18.8 3.2 %all-gather.3 = s32[2,4,128]{2,1,0:T(4,128)S(1)} all-gather(s32[1,4,128]{2,1,0:T(4,128)S(1)} %fusion.120), channel_id=1, replica_groups=mesh['tm'=16,'doc'=2] {'doc'}, dimensions={0}, use_global_device_ids=true | all-gather | bytes 6144 | tf_op jit(solution)/shard_map/all_gather | solution.py:61
  22.0 2.8 %gather_fusion.1 = f32[1024,128]{1,0:T(8,128)S(1)} fusion(f32[2048,128]{1,0:T(8,128)S(1)} %bitcast.257, s32[1024]{0:T(1024)S(1)} %broadcast_clamp_fusion), kind=kCustom, calls=%fused_computation.1 | custom fusion | bytes 1052672 | tf_op jit(solution)/shard_map/jit(_take)/gather | solution.py:71
  24.9 1.0 fusion.24
  25.9 3.2 %all-gather = s32[1,8,128]{2,0,1:T(1,128)S(1)} all-gather(s32[1,4,128]{2,0,1:T(1,128)S(1)} %bitcast.279), channel_id=2, replica_groups=mesh['tm'=16,'doc'=2] {'doc'}, dimensions={1}, use_global_device_ids=true | all-gather | bytes 6144 | tf_op jit(solution)/shard_map/all_gather | solution.py:62
  29.5 24.0 %all-reduce.2.cloned.1.call-done = bf16[1024,128]{1,0:T(8,128)(2,1)} async-done(((bf16[1024,128]{1,0:T(8,128)(2,1)}), bf16[1024,128]{1,0:T(8,128)(2,1)}) %all-reduce.2.cloned.1.call-update) | async-done | bytes 262160 | tf_op jit(solution)/shard_map/psum | solution.py:75
  53.5 1.2 fusion.6
  54.7 1.3 fusion.23
  56.1 1.4 multiply_reduce_fusion.3
  57.5 1.2 fusion.8
  61.9 2.8 %fusion.4 = f32[2048,128]{1,0:T(8,128)} fusion(bf16[1024,128]{1,0:T(8,128)(2,1)S(1)} %fusion.17, s32[1024]{0:T(1024)S(1)} %bitcast.274, f32[1,2048,128]{2,1,0:T(8,128)S(1)} %copy-done.2), kind=kOutput, calls=%fused_computation.11 | convolution fusion | flops 539230208 | bytes 2363392 | tf_op jit(solution)/shard_map/dot_general | solution.py:81
  64.7 7.0 %all-to-all-start = ((f32[16,128,128]{2,1,0:T(8,128)}), f32[16,128,128]{2,1,0:T(8,128)S(1)}, u32[]{:S(2)}, u32[]{:S(2)}) async-start(f32[16,128,128]{2,1,0:T(8,128)} %bitcast.59), calls=%async_computation | async-start | bytes 2097152 | tf_op jit(solution)/shard_map/all_to_all | solution.py:89
  71.7 12.5 %while.16 = (s32[]{:T(128)}, f32[128]{0:T(128)S(1)}, f32[16,128]{1,0:T(8,128)S(1)}, f32[16,128]{1,0:T(8,128)S(1)}, f32[16,128]{1,0:T(8,128)}, /*index=5*/f32[128]{0:T(128)S(1)}, s32[]{:T(128)}, s32[]{:T(128)}) while((s32[]{:T(128)}, f32[128]{0:T(128)S(1)}, f32[16,128]{1,0:T(8,128)S(1)}, f32[16,128]{1,0:T(8,128)S(1)}, ...), condition=%wide.region_1.0_spmd.clone, body=%wide.region_0.0_spmd.clone.sunk | while | flops 771 | bytes 5235 | solution.py:21
  71.7 0.7 fusion.137
  72.5 0.7 fusion.137
  73.3 0.7 fusion.137
  84.3 12.3 %all-to-all-done = f32[16,128,128]{2,1,0:T(8,128)S(1)} async-done(((f32[16,128,128]{2,1,0:T(8,128)}), f32[16,128,128]{2,1,0:T(8,128)S(1)}, u32[]{:S(2)}, u32[]{:S(2)}) %all-to-all-start) | async-done | bytes 1048608 | tf_op jit(solution)/shard_map/all_to_all | solution.py:89
  96.6 0.9 add_dynamic-update-slice_fusion
  107.1 4.8 %all-to-all-start.1 = ((f32[16,128,128]{2,1,0:T(8,128)}), f32[16,128,128]{2,1,0:T(8,128)S(1)}, u32[]{:S(2)}, u32[]{:S(2)}) async-start(f32[16,128,128]{2,1,0:T(8,128)} %fusion.41), calls=%async_computation.1 | async-start | bytes 2097152 | tf_op jit(solution)/shard_map/all_to_all | solution.py:111
  113.0 23.8 %all-to-all-done.1 = f32[16,128,128]{2,1,0:T(8,128)S(1)} async-done(((f32[16,128,128]{2,1,0:T(8,128)}), f32[16,128,128]{2,1,0:T(8,128)S(1)}, u32[]{:S(2)}, u32[]{:S(2)}) %all-to-all-start.1) | async-done | bytes 1048608 | tf_op jit(solution)/shard_map/all_to_all | solution.py:111
  136.8 1.0 copy.43
  (113 shorter events, 24.8 us)
Async XLA Ops:
  7.2 8.2 %copy-start = (s32[32]{0:T(128)S(1)}, s32[32]{0:T(128)}, u32[]{:S(2)}) copy-start(s32[32]{0:T(128)} %param.14) | copy-start | bytes 388
  7.2 1.7 %copy-start.2 = (f32[1,2048,128]{2,1,0:T(8,128)S(1)}, f32[1,2048,128]{2,1,0:T(8,128)}, u32[]{:S(2)}) copy-start(f32[1,2048,128]{2,1,0:T(8,128)} %param.11) | copy-start | bytes 3145732
  7.2 46.3 %all-reduce.2.cloned.1.call-start = ((), (), s32[]{:S(2)}) async-start(), calls=%async_computation.2 | async-start | bytes 524288 | tf_op jit(solution)/shard_map/psum | solution.py:75
  7.2 8.1 %copy-start.5 = (s32[1,4,128]{2,1,0:T(4,128)S(1)}, s32[1,4,128]{2,1,0:T(4,128)}, u32[]{:S(2)}) copy-start(s32[1,4,128]{2,1,0:T(4,128)} %param.12) | copy-start | bytes 6148
  24.8 1.1 copy-start.6
  24.8 4.5 %copy-start.4 = (f32[128]{0:T(128)S(1)}, f32[128]{0:T(128)}, u32[]{:S(2)}) copy-start(f32[128]{0:T(128)} %param.15) | copy-start | bytes 1540
  53.5 5.2 %copy-start.1 = (bf16[1024,128]{1,0:T(8,128)(2,1)S(1)}, bf16[1024,128]{1,0:T(8,128)(2,1)}, u32[]{:S(2)}) copy-start(bf16[1024,128]{1,0:T(8,128)(2,1)} %all-reduce.2.cloned.1.call-done) | copy-start | bytes 786436
  64.7 7.0 %copy-start.3 = (f32[128]{0:T(128)S(1)}, f32[128]{0:T(128)}, u32[]{:S(2)}) copy-start(f32[128]{0:T(128)} %param.16) | copy-start | bytes 1540
  64.7 31.9 %all-to-all-start = ((f32[16,128,128]{2,1,0:T(8,128)}), f32[16,128,128]{2,1,0:T(8,128)S(1)}, u32[]{:S(2)}, u32[]{:S(2)}) async-start(f32[16,128,128]{2,1,0:T(8,128)} %bitcast.59), calls=%async_computation | async-start | bytes 2097152 | tf_op jit(solution)/shard_map/all_to_all | solution.py:89
  107.1 29.7 %all-to-all-start.1 = ((f32[16,128,128]{2,1,0:T(8,128)}), f32[16,128,128]{2,1,0:T(8,128)S(1)}, u32[]{:S(2)}, u32[]{:S(2)}) async-start(f32[16,128,128]{2,1,0:T(8,128)} %fusion.41), calls=%async_computation.1 | async-start | bytes 2097152 | tf_op jit(solution)/shard_map/all_to_all | solution.py:111
Sparse Core Ops, SparseCore 0:
  26.0 27.4 all-reduce.1
where the time goes:
time: 146 us; the launch traced here: 145 us
  waiting for transfers between devices  60.2 us (41%)
  other arithmetic  29.6 us (20%)
  between operations  14.3 us (10%)
  local copies, waits for them, and re-layouts  13.1 us (9%)
  blocking collectives  12.6 us (9%)
  starting transfers between devices  11.8 us (8%)
  matrix products  2.76 us (2%)
    psum x1, waiting for transfers between devices, body(): lax.psum(partial, 'doc')  24 us
    all_to_all x1, waiting for transfers between devices, body(): lax.all_to_all(smoothed, 'tm', split_axis=0, concat_axis=0, tiled=True)  23.8 us
    all_to_all x1, waiting for transfers between devices, body(): lax.all_to_all(pseudo.reshape(years, chunk, topics), 'tm', split_axis=0,...  12.3 us
    add x16, other arithmetic, forward_step(): return (filt_var + drift_var, (gain_now, filt_var))  11.4 us
    all_to_all x1, starting transfers between devices, body(): lax.all_to_all(pseudo.reshape(years, chunk, topics), 'tm', split_axis=0,...  6.99 us
    unnamed x22, local copies, waits for them, and re-layouts  5.44 us
    unnamed x10, other arithmetic  5.43 us
    all_to_all x1, starting transfers between devices, body(): lax.all_to_all(smoothed, 'tm', split_axis=0, concat_axis=0, tiled=True)  4.76 us
  transfers between devices with their start and end apart: 3, of which 3 were waited for; matrix products, arithmetic and copies ran while one was open for 9% of the time, Pallas kernels for 0%

commit v1 on v0

--- a/solution.py
+++ b/solution.py
@@ -58,7 +58,11 @@
     local_docs = slot_ids.shape[0]
     slot_width = slot_ids.shape[1]
     columns = jnp.take(block_slot, slot_ids // BLOCK) * BLOCK + slot_ids % BLOCK
-    all_columns = lax.all_gather(columns, "doc", axis=0, tiled=True)
+    n_lanes = jax.lax.axis_size("doc")
+    vals = [n_lanes if kk == 0 else 1 for kk in range(columns.ndim)]
+    all_columns = jax.lax.all_to_all(
+        jnp.tile(columns, vals), "doc", split_axis=0, concat_axis=0, tiled=True
+    )
     all_counts = lax.all_gather(word_counts[0], "doc", axis=0, tiled=True)
     peaks = lax.all_gather(local_peak, "doc")
     totals = lax.all_gather(local_total, "doc")

time: 146 us -> 149 us (1.021)
  waiting for transfers between devices: 60.2 us -> 64 us
  blocking collectives: 12.6 us -> 9.36 us
  starting transfers between devices: 11.8 us -> 15 us
    psum x1, waiting for transfers between devices: 24 us -> 27.8 us  [body(): lax.psum(partial, 'doc')]
    all_to_all x0 -> x1, starting transfers between devices: none -> 3.22 us  [body(): jax.lax.all_to_all(jnp.tile(columns, vals), 'doc', split_axis=0, concat_a...]
    all_gather x1 -> x0, blocking collectives: 3.21 us -> none  [body(): all_columns = lax.all_gather(columns, 'doc', axis=0, tiled=True)]
    unnamed x10 -> x9, other arithmetic: 5.43 us -> 5.42 us
  transfers between devices with their start and end apart: 3 -> 4, of which waited for: 3 -> 3; matrix products, arithmetic and copies ran while one was open for 9% -> 10% of each run, Pallas kernels for 0% -> 0%
where the time goes in v1:
time: 149 us; the launch traced here: 148 us
  waiting for transfers between devices  64 us (43%)
  other arithmetic  29 us (19%)
  starting transfers between devices  15 us (10%)
  between operations  14.4 us (10%)
  local copies, waits for them, and re-layouts  13.7 us (9%)
  blocking collectives  9.36 us (6%)
  matrix products  2.76 us (2%)
    psum x1, waiting for transfers between devices, body(): lax.psum(partial, 'doc')  27.8 us
    all_to_all x1, waiting for transfers between devices, body(): lax.all_to_all(smoothed, 'tm', split_axis=0, concat_axis=0, tiled=True)  23.8 us
    all_to_all x1, waiting for transfers between devices, body(): lax.all_to_all(pseudo.reshape(years, chunk, topics), 'tm', split_axis=0,...  12.3 us
    add x16, other arithmetic, forward_step(): return (filt_var + drift_var, (gain_now, filt_var))  11.3 us
    all_to_all x1, starting transfers between devices, body(): lax.all_to_all(pseudo.reshape(years, chunk, topics), 'tm', split_axis=0,...  6.99 us
    unnamed x22, local copies, waits for them, and re-layouts  5.45 us
    unnamed x9, other arithmetic  5.42 us
    all_to_all x1, starting transfers between devices, body(): lax.all_to_all(smoothed, 'tm', split_axis=0, concat_axis=0, tiled=True)  4.76 us
  transfers between devices with their start and end apart: 4, of which 3 were waited for; matrix products, arithmetic and copies ran while one was open for 10% of the time, Pallas kernels for 0%

profile of v1, /device:TPU:9, one launch (start us, length us, event | category | flops | bytes accessed | tf_op | source)
XLA Modules:
  0.0 148.4 jit_solution(9539119454600555135)
XLA Ops:
  7.9 3.3 %gather_fusion = s32[512]{0:T(512)S(1)} fusion(s32[32]{0:T(128)S(1)} %copy-done, s32[1024]{0:T(1024)S(1)} %pad_clamp_fusion), kind=kCustom, calls=%fused_computation | custom fusion | bytes 6144 | tf_op jit(solution)/shard_map/jit(_take)/gather | solution.py:60
  11.9 3.2 %all-to-all-start = ((s32[2,4,128]{2,1,0:T(4,128)}), s32[2,4,128]{2,1,0:T(4,128)S(1)}, u32[]{:S(2)}, u32[]{:S(2)}) async-start(s32[2,4,128]{2,1,0:T(4,128)} %tile.2), calls=%async_computation | async-start | bytes 8192 | tf_op jit(solution)/shard_map/all_to_all | solution.py:63
  15.8 3.1 %all-gather.4 = f32[2,1,128]{2,1,0:T(1,128)S(1)} all-gather(f32[1,1,128]{2,1,0:T(1,128)S(1)} %bitcast.279), channel_id=4, replica_groups=mesh['tm'=16,'doc'=2] {'doc'}, dimensions={0}, use_global_device_ids=true | all-gather | bytes 1536 | tf_op jit(solution)/shard_map/all_gather | solution.py:68
  18.9 3.1 %all-gather.3 = f32[2,1,128]{2,1,0:T(1,128)S(1)} all-gather(f32[1,1,128]{2,1,0:T(1,128)S(1)} %bitcast.276), channel_id=3, replica_groups=mesh['tm'=16,'doc'=2] {'doc'}, dimensions={0}, use_global_device_ids=true | all-gather | bytes 1536 | tf_op jit(solution)/shard_map/all_gather | solution.py:67
  22.0 3.2 %all-gather = s32[1,8,128]{2,0,1:T(1,128)S(1)} all-gather(s32[1,4,128]{2,0,1:T(1,128)S(1)} %bitcast.277), channel_id=2, replica_groups=mesh['tm'=16,'doc'=2] {'doc'}, dimensions={1}, use_global_device_ids=true | all-gather | bytes 6144 | tf_op jit(solution)/shard_map/all_gather | solution.py:66
  25.4 2.8 %gather_fusion.1 = f32[1024,128]{1,0:T(8,128)S(1)} fusion(f32[2048,128]{1,0:T(8,128)S(1)} %bitcast.255, s32[1024]{0:T(1024)S(1)} %broadcast_clamp_fusion), kind=kCustom, calls=%fused_computation.1 | custom fusion | bytes 1052672 | tf_op jit(solution)/shard_map/jit(_take)/gather | solution.py:75
  28.2 1.0 fusion.24
  29.5 27.8 %all-reduce.2.cloned.1.call-done = bf16[1024,128]{1,0:T(8,128)(2,1)} async-done(((bf16[1024,128]{1,0:T(8,128)(2,1)}), bf16[1024,128]{1,0:T(8,128)(2,1)}) %all-reduce.2.cloned.1.call-update) | async-done | bytes 262160 | tf_op jit(solution)/shard_map/psum | solution.py:79
  57.3 1.2 fusion.6
  58.5 1.3 fusion.23
  59.8 1.4 multiply_reduce_fusion.3
  61.3 1.2 fusion.8
  65.7 2.8 %fusion.4 = f32[2048,128]{1,0:T(8,128)} fusion(bf16[1024,128]{1,0:T(8,128)(2,1)S(1)} %fusion.17, s32[1024]{0:T(1024)S(1)} %bitcast.272, f32[1,2048,128]{2,1,0:T(8,128)S(1)} %copy-done.2), kind=kOutput, calls=%fused_computation.11 | convolution fusion | flops 539230208 | bytes 2363392 | tf_op jit(solution)/shard_map/dot_general | solution.py:85
  68.5 7.0 %all-to-all-start.1 = ((f32[16,128,128]{2,1,0:T(8,128)}), f32[16,128,128]{2,1,0:T(8,128)S(1)}, u32[]{:S(2)}, u32[]{:S(2)}) async-start(f32[16,128,128]{2,1,0:T(8,128)} %bitcast.58), calls=%async_computation.1 | async-start | bytes 2097152 | tf_op jit(solution)/shard_map/all_to_all | solution.py:93
  75.5 12.5 %while.16 = (s32[]{:T(128)}, f32[128]{0:T(128)S(1)}, f32[16,128]{1,0:T(8,128)S(1)}, f32[16,128]{1,0:T(8,128)S(1)}, f32[16,128]{1,0:T(8,128)}, /*index=5*/f32[128]{0:T(128)S(1)}, s32[]{:T(128)}, s32[]{:T(128)}) while((s32[]{:T(128)}, f32[128]{0:T(128)S(1)}, f32[16,128]{1,0:T(8,128)S(1)}, f32[16,128]{1,0:T(8,128)S(1)}, ...), condition=%wide.region_1.0_spmd.clone, body=%wide.region_0.0_spmd.clone.sunk | while | flops 771 | bytes 5235 | solution.py:21
  76.3 0.7 fusion.136
  77.1 0.7 fusion.136
  78.6 0.7 fusion.136
  79.4 0.7 fusion.136
  88.1 12.3 %all-to-all-done.1 = f32[16,128,128]{2,1,0:T(8,128)S(1)} async-done(((f32[16,128,128]{2,1,0:T(8,128)}), f32[16,128,128]{2,1,0:T(8,128)S(1)}, u32[]{:S(2)}, u32[]{:S(2)}) %all-to-all-start.1) | async-done | bytes 1048608 | tf_op jit(solution)/shard_map/all_to_all | solution.py:93
  100.4 0.9 add_dynamic-update-slice_fusion
  110.9 4.8 %all-to-all-start.2 = ((f32[16,128,128]{2,1,0:T(8,128)}), f32[16,128,128]{2,1,0:T(8,128)S(1)}, u32[]{:S(2)}, u32[]{:S(2)}) async-start(f32[16,128,128]{2,1,0:T(8,128)} %fusion.41), calls=%async_computation.2 | async-start | bytes 2097152 | tf_op jit(solution)/shard_map/all_to_all | solution.py:115
  116.8 23.8 %all-to-all-done.2 = f32[16,128,128]{2,1,0:T(8,128)S(1)} async-done(((f32[16,128,128]{2,1,0:T(8,128)}), f32[16,128,128]{2,1,0:T(8,128)S(1)}, u32[]{:S(2)}, u32[]{:S(2)}) %all-to-all-start.2) | async-done | bytes 1048608 | tf_op jit(solution)/shard_map/all_to_all | solution.py:115
  140.6 1.0 copy.43
  (115 shorter events, 25.6 us)
Async XLA Ops:
  7.2 0.7 copy-start
  7.9 3.4 %copy-start.5 = (s32[1,4,128]{2,1,0:T(4,128)S(1)}, s32[1,4,128]{2,1,0:T(4,128)}, u32[]{:S(2)}) copy-start(s32[1,4,128]{2,1,0:T(4,128)} %param.12) | copy-start | bytes 6148
  7.9 7.3 %copy-start.2 = (f32[1,2048,128]{2,1,0:T(8,128)S(1)}, f32[1,2048,128]{2,1,0:T(8,128)}, u32[]{:S(2)}) copy-start(f32[1,2048,128]{2,1,0:T(8,128)} %param.11) | copy-start | bytes 3145732
  11.9 13.4 %all-to-all-start = ((s32[2,4,128]{2,1,0:T(4,128)}), s32[2,4,128]{2,1,0:T(4,128)S(1)}, u32[]{:S(2)}, u32[]{:S(2)}) async-start(s32[2,4,128]{2,1,0:T(4,128)} %tile.2), calls=%async_computation | async-start | bytes 8192 | tf_op jit(solution)/shard_map/all_to_all | solution.py:63
  15.1 6.9 %copy-start.6 = (s32[1,4,128]{2,1,0:T(4,128)S(1)}, s32[1,4,128]{2,1,0:T(4,128)}, u32[]{:S(2)}) copy-start(s32[1,4,128]{2,1,0:T(4,128)} %param.13) | copy-start | bytes 6148
  15.1 42.2 %all-reduce.2.cloned.1.call-start = ((), (), s32[]{:S(2)}) async-start(), calls=%async_computation.3 | async-start | bytes 524288 | tf_op jit(solution)/shard_map/psum | solution.py:79
  28.2 1.1 copy-start.4
  57.3 5.2 %copy-start.1 = (bf16[1024,128]{1,0:T(8,128)(2,1)S(1)}, bf16[1024,128]{1,0:T(8,128)(2,1)}, u32[]{:S(2)}) copy-start(bf16[1024,128]{1,0:T(8,128)(2,1)} %all-reduce.2.cloned.1.call-done) | copy-start | bytes 786436
  68.5 7.0 %copy-start.3 = (f32[128]{0:T(128)S(1)}, f32[128]{0:T(128)}, u32[]{:S(2)}) copy-start(f32[128]{0:T(128)} %param.16) | copy-start | bytes 1540
  68.5 31.9 %all-to-all-start.1 = ((f32[16,128,128]{2,1,0:T(8,128)}), f32[16,128,128]{2,1,0:T(8,128)S(1)}, u32[]{:S(2)}, u32[]{:S(2)}) async-start(f32[16,128,128]{2,1,0:T(8,128)} %bitcast.58), calls=%async_computation.1 | async-start | bytes 2097152 | tf_op jit(solution)/shard_map/all_to_all | solution.py:93
  110.9 29.7 %all-to-all-start.2 = ((f32[16,128,128]{2,1,0:T(8,128)}), f32[16,128,128]{2,1,0:T(8,128)S(1)}, u32[]{:S(2)}, u32[]{:S(2)}) async-start(f32[16,128,128]{2,1,0:T(8,128)} %fusion.41), calls=%async_computation.2 | async-start | bytes 2097152 | tf_op jit(solution)/shard_map/all_to_all | solution.py:115
Sparse Core Ops, SparseCore 0:
  29.4 27.8 all-reduce.1
